TPU v7x, 32 devices: a whole 2x2x4 slice. The times are simulated.
32 devices in a mesh: groups: 1, orb: 32 (over z, y, x, core), aux: 1.
Axes of the slice: x: 2, y: 2, z: 4, core: 2. Of those that a mesh axis runs over, the one named last changes fastest.
Arguments:
- exchange_integral_halves: float32 [1, 128, 256, 256], P('aux', ('groups', 'orb')), may hold values from -3 to 3
- amplitudes: bfloat16 [128, 256, 256], P(('groups', 'orb')), may hold values from -6 to 6
- pair_slot_orbitals: int32 [128, 2], P('groups'), may hold values from 0 to 63
- pao_domain: int32 [64, 256], P('groups'), may hold values from 0 to 511, as said below
- pao_intersection: bfloat16 [512, 512], P('groups'), as said below
- pao_fock: bfloat16 [512, 512], P('groups'), as said below
- occ_energy: float32 [64], P('groups'), may hold values from -1.5 to -0.3
- coupled_pair_owner: int32 [128, 8], P(('groups', 'orb')), may hold values from 0 to 31, all different within a row; in each aligned block of 4 rows (0 to 3, 4 to 7, ...) at most 2 rows name the same one
- coupled_pair_slot: int32 [128, 8], P(('groups', 'orb')), may hold values from 0 to 3
- coupling_swap_flag: int32 [128, 8], P(('groups', 'orb')), may hold values from 0 to 1
- coupling_fock_element: float32 [128, 8], P(('groups', 'orb')), may hold values from -1.2 to 1.2
Outputs:
- residual: float32 [128, 256, 256], P(('groups', 'orb'), 'aux')
- updated_pair_amplitudes: bfloat16 [128, 256, 256], P(('groups', 'orb'), 'aux')
Inputs may be any that keep to these rules, and one draw needn't show every extreme that they name: `pao_domain`: each orbital's 256 domain entries are distinct. `coupled_pair_owner`: the 8 owners in one row differ; among the 4 pair slots of one owner no owner is named by more than 2 rows, a bound that some block reaches. `pao_intersection`: symmetric with unit diagonal. `pao_fock`: symmetric with diagonal from 0.5 to 3.
All inputs are finite; a program needn't handle non-finite values.
Results may differ from a plain program's by a relative error of at most 0.012.
Values may be sent and summed in bfloat16 or wider, within the bound.
No kernel may reach another device: no remote copies, remote signals or barrier semaphores. Data moves between devices by JAX's collectives and lax.ppermute only.
A program may use at most 128 MiB of HBM per device.

v0:
```python
import jax
import jax.numpy as jnp
from jax import lax
from jax.sharding import PartitionSpec as P


def one_hot(ids, width):
    return (ids[..., None] == jnp.arange(width, dtype=ids.dtype)).astype(jnp.bfloat16)


def sel_rows(onehot, matrix):
    return jnp.einsum("...rk,kc->...rc", onehot, matrix, preferred_element_type=jnp.float32).astype(
        jnp.bfloat16
    )


def shards(
    exchange_integral_halves,
    amplitudes,
    pair_slot_orbitals,
    pao_domain,
    pao_intersection,
    pao_fock,
    occ_energy,
    coupled_pair_owner,
    coupled_pair_slot,
    coupling_swap_flag,
    coupling_fock_element,
):
    slot_count, extent = (amplitudes.shape[0], amplitudes.shape[1])
    paos = pao_intersection.shape[0]
    halves = lax.axis_size("aux")
    owner_index = lax.axis_index("orb")
    aux_index = lax.axis_index("aux")
    half_rows = extent // halves
    row_first = aux_index * half_rows
    every_amp = lax.all_gather(amplitudes, "orb", axis=0, tiled=True)
    own_slots = owner_index * slot_count + jnp.arange(slot_count, dtype=jnp.int32)
    orb_i = pair_slot_orbitals[own_slots, 0]
    orb_j = pair_slot_orbitals[own_slots, 1]
    dom_i = pao_domain[orb_i]
    dom_j = pao_domain[orb_j]
    rows_dom = lax.dynamic_slice_in_dim(dom_i, row_first, half_rows, 1)
    energy_sum = occ_energy[orb_i] + occ_energy[orb_j]
    global_slot = coupled_pair_owner * slot_count + coupled_pair_slot
    flipped = coupling_swap_flag == 1
    first_orb = pair_slot_orbitals[global_slot, 0]
    second_orb = pair_slot_orbitals[global_slot, 1]
    orb_p = jnp.where(flipped, second_orb, first_orb)
    orb_q = jnp.where(flipped, first_orb, second_orb)
    oh_rows = one_hot(rows_dom, paos)
    oh_i = one_hot(dom_i, paos)
    oh_j = one_hot(dom_j, paos)
    oh_p = one_hot(pao_domain[orb_p], paos)
    oh_q = one_hot(pao_domain[orb_q], paos)
    rs = sel_rows(oh_rows, pao_intersection)
    rf = sel_rows(oh_rows, pao_fock)
    s_ii = jnp.einsum("brk,bak->bra", rs, oh_i, preferred_element_type=jnp.float32).astype(
        jnp.bfloat16
    )
    f_ii = jnp.einsum("brk,bak->bra", rf, oh_i, preferred_element_type=jnp.float32).astype(
        jnp.bfloat16
    )
    js = sel_rows(oh_j, pao_intersection)
    jf = sel_rows(oh_j, pao_fock)
    s_jj = jnp.einsum("bjk,bak->bja", js, oh_j, preferred_element_type=jnp.float32).astype(
        jnp.bfloat16
    )
    f_jj = jnp.einsum("bjk,bak->bja", jf, oh_j, preferred_element_type=jnp.float32).astype(
        jnp.bfloat16
    )
    col_s = jnp.einsum(
        "kc,bjc->bkj", pao_intersection, oh_j, preferred_element_type=jnp.float32
    ).astype(jnp.bfloat16)
    s_ip = jnp.einsum("brk,bcpk->bcrp", rs, oh_p, preferred_element_type=jnp.float32).astype(
        jnp.bfloat16
    )
    s_qj = jnp.einsum("bcqk,bkj->bcqj", oh_q, col_s, preferred_element_type=jnp.float32).astype(
        jnp.bfloat16
    )
    summed = lax.psum_scatter(exchange_integral_halves[0], "aux", scatter_dimension=1, tiled=True)
    left_f = jnp.einsum(
        "bra,bad->brd", f_ii, amplitudes, preferred_element_type=jnp.float32
    ).astype(jnp.bfloat16)
    left_s = jnp.einsum(
        "bra,bad->brd", s_ii, amplitudes, preferred_element_type=jnp.float32
    ).astype(jnp.bfloat16)
    summed = summed + jnp.einsum("brd,bdj->brj", left_f, s_jj, preferred_element_type=jnp.float32)
    summed = summed + jnp.einsum("brd,bdj->brj", left_s, f_jj, preferred_element_type=jnp.float32)
    summed = summed - energy_sum[:, None, None] * jnp.einsum(
        "brd,bdj->brj", left_s, s_jj, preferred_element_type=jnp.float32
    )
    blocks = every_amp[global_slot]
    blocks = jnp.where(flipped[:, :, None, None], jnp.swapaxes(blocks, 2, 3), blocks)
    reach = jnp.einsum("bcrp,bcpd->bcrd", s_ip, blocks, preferred_element_type=jnp.float32).astype(
        jnp.bfloat16
    )
    for column in range(coupled_pair_owner.shape[1]):
        summed = summed - coupling_fock_element[:, column][:, None, None] * jnp.einsum(
            "brd,bdj->brj", reach[:, column], s_qj[:, column], preferred_element_type=jnp.float32
        )
    pao_energy = jnp.diagonal(pao_fock).astype(jnp.float32)
    denom = (
        pao_energy[rows_dom][:, :, None] + pao_energy[dom_j][:, None, :] - energy_sum[:, None, None]
    )
    amp_rows = lax.dynamic_slice_in_dim(amplitudes, row_first, half_rows, 1).astype(jnp.float32)
    updated = (amp_rows - summed / denom).astype(jnp.bfloat16)
    return (summed, updated)


def solution(mesh):
    placed = (
        P("aux", ("groups", "orb"), None, None),
        P(("groups", "orb"), None, None),
        P("groups", None),
        P("groups", None),
        P("groups", None),
        P("groups", None),
        P("groups"),
        P(("groups", "orb"), None),
        P(("groups", "orb"), None),
        P(("groups", "orb"), None),
        P(("groups", "orb"), None),
    )
    return jax.shard_map(
        shards,
        mesh=mesh,
        in_specs=placed,
        out_specs=(P(("groups", "orb"), "aux", None), P(("groups", "orb"), "aux", None)),
        check_vma=False,
    )
```

profile of v0, /device:TPU:0, one launch (start us, length us, event | category | flops | bytes accessed | tf_op | source)
XLA Modules:
  0.0 166.4 jit_solution(18155204422644652714)
XLA Ops:
  7.2 0.7 all-gather.2.cloned.1.call-update
  7.9 1.3 gather_fusion.2
  9.3 1.3 gather_fusion
  10.6 1.3 gather_fusion.4
  11.9 1.4 gather_fusion.1
  13.3 1.3 gather_fusion.5
  14.6 1.4 gather_fusion.3
  16.0 8.0 %gather_fusion.11 = bf16[512]{0:T(512)(128)(2,1)S(1)} fusion(bf16[512,512]{1,0:T(8,128)(2,1)} %param.16, s32[512]{0:T(512)S(1)} %bitcast.130), kind=kCustom, calls=%fused_computation.11 | custom fusion | bytes 6144 | tf_op jit(solution)/shard_map/jit(diagonal)/cond/branch_0_fun/gather | solution.py:102
  24.1 6.9 %gather_fusion.13 = f32[1024]{0:T(1024)S(1)} fusion(f32[512]{0:T(512)S(1)} %convert_element_type.73, s32[1024]{0:T(1024)S(1)} %broadcast_clamp_fusion), kind=kCustom, calls=%fused_computation.13 | custom fusion | bytes 12288 | tf_op jit(solution)/shard_map/gather | solution.py:104
  31.1 6.9 %gather_fusion.12 = f32[1024]{0:T(1024)S(1)} fusion(f32[512]{0:T(512)S(1)} %convert_element_type.73, s32[1024]{0:T(1024)S(1)} %broadcast_clamp_fusion.1), kind=kCustom, calls=%fused_computation.12 | custom fusion | bytes 12288 | tf_op jit(solution)/shard_map/gather | solution.py:104
  38.1 0.8 gather_fusion.6
  39.0 0.8 gather_fusion.7
  40.2 0.6 gather_fusion.10
  40.8 0.6 gather_fusion.8
  41.7 1.7 %fusion.28.clone.5 = bf16[4,256,512,1]{2,1,3,0:T(8,128)(2,1)} fusion(s32[4,256]{1,0:T(4,128)S(1)} %gather_fusion.3, bf16[512,512]{1,0:T(8,128)(2,1)S(1)} %copy-done), kind=kOutput, calls=%fused_computation.42.clone.clone.clone.2 | convolution fusion | flops 537919488 | bytes 1576960 | tf_op jit(solution)/shard_map/kc,bjc->bkj/dot_general | solution.py:72
  43.5 1.1 fusion.40
  44.6 1.9 %fusion.41 = bf16[4,256,256]{2,1,0:T(8,128)(2,1)} fusion(s32[4,256]{1,0:T(4,128)S(1)} %gather_fusion.3, bf16[512,512]{1,0:T(8,128)(2,1)S(1)} %copy-done.6), kind=kOutput, calls=%fused_computation.66 | convolution fusion | flops 807141376 | bytes 1052672 | tf_op jit(solution)/shard_map/bjk,bak->bja/dot_general | solution.py:69
  46.5 1.9 %fusion.38 = bf16[4,256,256]{2,1,0:T(8,128)(2,1)} fusion(s32[4,256]{1,0:T(4,128)S(1)} %gather_fusion.1, bf16[512,512]{1,0:T(8,128)(2,1)S(1)} %copy-done.6), kind=kOutput, calls=%fused_computation.63 | convolution fusion | flops 807141376 | bytes 1052672 | tf_op jit(solution)/shard_map/brk,bak->bra/dot_general | solution.py:61
  48.4 1.7 %fusion.24 = bf16[4,256,512]{2,1,0:T(8,128)(2,1)} fusion(s32[4,256]{1,0:T(4,128)S(1)} %gather_fusion.1, bf16[512,512]{1,0:T(8,128)(2,1)S(1)} %copy-done), kind=kOutput, calls=%fused_computation.38 | convolution fusion | flops 537919488 | bytes 1576960 | tf_op jit(solution)/shard_map/...rk,kc->...rc/dot_general | solution.py:12
  50.2 2.0 %convolution_convert_fusion = bf16[4,256,256]{2,1,0:T(8,128)(2,1)S(1)} fusion(bf16[4,256,256]{2,1,0:T(8,128)(2,1)S(1)} %copy-done.5, bf16[4,256,512]{2,1,0:T(8,128)(2,1)} %fusion.24, s32[4,256]{1,0:T(4,128)S(1)} %gather_fusion.1), kind=kOutput, calls=%fused_computation.67 | convolution fusion | flops 403701760 | bytes 2101248 | tf_op jit(solution)/shard_map/bra,bad->brd/dot_general | solution.py:85
  52.2 1.8 %convolution_add_fusion.1 = f32[4,256,256]{2,1,0:T(8,128)S(1)} fusion(bf16[4,256,256]{2,1,0:T(8,128)(2,1)S(1)} %fusion.40, bf16[4,256,256]{2,1,0:T(8,128)(2,1)} %fusion.38, bf16[4,256,256]{2,1,0:T(8,128)(2,1)S(1)} %copy-done.5, f32[1,4,256,256]{3,2,1,0:T(8,128)} %param.11), kind=kOutput, calls=%fused_computation.62 | convolution fusion | flops 268959744 | bytes 3670016 | tf_op jit(solution)/shard_map/brd,bdj->brj/dot_general | solution.py:88
  54.1 1.4 convolution_add_fusion
  55.8 4.6 %fusion.13 = bf16[4,8,256,256]{3,2,1,0:T(8,128)(2,1)} fusion(s32[4,8,256]{2,1,0:T(8,128)S(1)} %bitcast.134, bf16[4,256,512,1]{2,1,3,0:T(8,128)(2,1)S(1)} %copy-done.12), kind=kOutput, calls=%fused_computation.25 | convolution fusion | flops 2153775104 | bytes 5275648 | tf_op jit(solution)/shard_map/bcqk,bkj->bcqj/dot_general | solution.py:78
  60.4 68.1 %all-gather.2.cloned.1.call-done = bf16[128,256,256]{2,1,0:T(8,128)(2,1)} async-done(((bf16[4,256,256]{2,1,0:T(8,128)(2,1)}), bf16[128,256,256]{2,1,0:T(8,128)(2,1)}) %all-gather.2.cloned.1.call-update) | async-done | bytes 16777232 | tf_op jit(solution)/shard_map/all_gather | solution.py:37
  128.5 8.6 %gather_fusion.9 = bf16[32,256,256]{2,1,0:T(8,128)(2,1)} fusion(bf16[128,256,256]{2,1,0:T(8,128)(2,1)} %all-gather.2.cloned.1.call-done, s32[1024]{0:T(1024)S(1)} %pad_clamp_fusion.1), kind=kCustom, calls=%fused_computation.9 | custom fusion | bytes 8388736 | tf_op jit(solution)/shard_map/gather | solution.py:93
  137.0 6.3 %copy.15 = bf16[4,8,256,256]{3,2,1,0:T(8,128)(2,1)} copy(bf16[4,8,256,256]{2,3,1,0:T(8,128)(2,1)} %bitcast.131) | data formatting | bytes 8388608 | tf_op jit(solution)/shard_map/transpose | solution.py:94
  143.3 8.1 %fusion.8 = bf16[4,8,256,256]{3,2,1,0:T(8,128)(2,1)} fusion(bf16[4,8,256,256]{3,2,1,0:T(8,128)(2,1)} %copy.15, bf16[4,8,256,256]{3,2,1,0:T(8,128)(2,1)} %bitcast.132, pred[4,8]{1,0:T(4,128)(4,1)S(1)} %get-tuple-element.11, s32[4,8,256]{2,1,0:T(8,128)S(1)} %bitcast.133, bf16[4,256,512]{2,1,0:T(8,128)(2,1)S(1)} %copy-done.11), kind=kOutput, calls=%fused_computation.24 | convolution fusion | flops 3231711232 | bytes 13664288 | tf_op jit(solution)/shard_map/bcrp,bcpd->bcrd/dot_general | solution.py:95
  151.4 1.7 fusion.36
  153.1 2.3 %fusion.35 = f32[4,256,256]{2,1,0:T(8,128)S(1)} fusion(f32[4,256,256]{2,1,0:T(8,128)S(1)} %fusion.36, bf16[4,8,256,256]{3,2,1,0:T(8,128)(2,1)} %fusion.13, bf16[4,8,256,256]{3,2,1,0:T(8,128)(2,1)} %fusion.8, f32[4]{0:T(128)S(1)} %get-tuple-element.7), kind=kOutput, calls=%fused_computation.56 | convolution fusion | flops 134742016 | bytes 3145744 | tf_op jit(solution)/shard_map/brd,bdj->brj/dot_general | solution.py:99
  155.3 1.4 fusion.34
  156.7 0.3 fusion.33
  158.0 1.6 subtract_convert_fusion
  (62 shorter events, 2.3 us)
Async XLA Ops:
  7.2 34.6 %copy-start = (bf16[512,512]{1,0:T(8,128)(2,1)S(1)}, bf16[512,512]{1,0:T(8,128)(2,1)}, u32[]{:S(2)}) copy-start(bf16[512,512]{1,0:T(8,128)(2,1)} %param.15) | copy-start | bytes 1572868
  7.2 121.3 %all-gather.2.cloned.1.call-start = ((), (), s32[]{:S(2)}) async-start(), calls=%async_computation | async-start | bytes 17301504 | tf_op jit(solution)/shard_map/all_gather | solution.py:37
  24.1 13.9 %copy-start.9 = (s32[4,8]{1,0:T(4,128)S(1)}, s32[4,8]{1,0:T(4,128)}, u32[]{:S(2)}) copy-start(s32[4,8]{1,0:T(4,128)} %param.19) | copy-start | bytes 388
  24.1 13.9 %copy-start.10 = (s32[4,8]{1,0:T(4,128)S(1)}, s32[4,8]{1,0:T(4,128)}, u32[]{:S(2)}) copy-start(s32[4,8]{1,0:T(4,128)} %param.18) | copy-start | bytes 388
  24.1 14.0 %copy-start.1 = (s32[128,2]{0,1:T(2,128)S(1)}, s32[128,2]{0,1:T(2,128)}, u32[]{:S(2)}) copy-start(s32[128,2]{0,1:T(2,128)} %param.13) | copy-start | bytes 3076
  31.1 8.9 %copy-start.8 = (s32[4,8]{1,0:T(4,128)S(1)}, s32[4,8]{1,0:T(4,128)}, u32[]{:S(2)}) copy-start(s32[4,8]{1,0:T(4,128)} %param.20) | copy-start | bytes 388
  31.1 9.1 %copy-start.2 = (s32[64,256]{1,0:T(8,128)S(1)}, s32[64,256]{1,0:T(8,128)}, u32[]{:S(2)}) copy-start(s32[64,256]{1,0:T(8,128)} %param.14) | copy-start | bytes 196612
  31.1 10.3 %copy-start.7 = (f32[4,8]{1,0:T(4,128)S(1)}, f32[4,8]{1,0:T(4,128)}, u32[]{:S(2)}) copy-start(f32[4,8]{1,0:T(4,128)} %param.21) | copy-start | bytes 388
  39.8 4.8 %copy-start.6 = (bf16[512,512]{1,0:T(8,128)(2,1)S(1)}, bf16[512,512]{1,0:T(8,128)(2,1)}, u32[]{:S(2)}) copy-start(bf16[512,512]{1,0:T(8,128)(2,1)} %param.16) | copy-start | bytes 1572868
  46.5 3.6 %copy-start.5 = (bf16[4,256,256]{2,1,0:T(8,128)(2,1)S(1)}, bf16[4,256,256]{2,1,0:T(8,128)(2,1)}, u32[]{:S(2)}) copy-start(bf16[4,256,256]{2,1,0:T(8,128)(2,1)} %param.12) | copy-start | bytes 1572868
  54.0 1.8 %copy-start.12 = (bf16[4,256,512,1]{2,1,3,0:T(8,128)(2,1)S(1)}, bf16[4,256,512,1]{2,1,3,0:T(8,128)(2,1)}, u32[]{:S(2)}) copy-start(bf16[4,256,512,1]{2,1,3,0:T(8,128)(2,1)} %fusion.28.clone.5) | copy-start | bytes 3145732
  137.0 6.3 %copy-start.11 = (bf16[4,256,512]{2,1,0:T(8,128)(2,1)S(1)}, bf16[4,256,512]{2,1,0:T(8,128)(2,1)}, u32[]{:S(2)}) copy-start(bf16[4,256,512]{2,1,0:T(8,128)(2,1)} %fusion.24) | copy-start | bytes 3145732
  151.4 3.9 %copy-start.3 = (bf16[4,8,256,256]{3,2,1,0:T(8,128)(2,1)S(1)}, bf16[4,8,256,256]{3,2,1,0:T(8,128)(2,1)}, u32[]{:S(2)}) copy-start(bf16[4,8,256,256]{3,2,1,0:T(8,128)(2,1)} %fusion.13) | copy-start | bytes 12582916
  151.4 5.3 %copy-start.4 = (bf16[4,8,256,256]{3,2,1,0:T(8,128)(2,1)S(1)}, bf16[4,8,256,256]{3,2,1,0:T(8,128)(2,1)}, u32[]{:S(2)}) copy-start(bf16[4,8,256,256]{3,2,1,0:T(8,128)(2,1)} %fusion.8) | copy-start | bytes 12582916
Sparse Core Ops, SparseCore 0:
  10.9 117.5 all-gather.1
where the time goes:
time: 167 us; the launch traced here: 166 us
  waiting for transfers between devices  68.8 us (41%)
  local copies, waits for them, and re-layouts  48.3 us (29%)
  matrix products  34.8 us (21%)
  between operations  14.4 us (9%)
    all_gather x1, waiting for transfers between devices, shards(): every_amp = lax.all_gather(amplitudes, 'orb', axis=0, tiled=True)  68.1 us
    gather x1, local copies, waits for them, and re-layouts, shards(): blocks = every_amp[global_slot]  8.55 us
    dot_general x8, matrix products, shards(): jnp.einsum('brd,bdj->brj', reach[:, column], s_qj[:, column], preferred_e...  8.1 us
    dot_general x1, matrix products, shards(): jnp.einsum('bcrp,bcpd->bcrd', s_ip, blocks, preferred_element_type=jnp.fl...  8.09 us
    gather x1, local copies, waits for them, and re-layouts, shards(): pao_energy = jnp.diagonal(pao_fock).astype(jnp.float32)  8.03 us
    gather x2, local copies, waits for them, and re-layouts, shards(): pao_energy[dom_j][:, None, :]  6.88 us
    gather x2, local copies, waits for them, and re-layouts, shards(): pao_energy[rows_dom][:, :, None] + pao_energy[dom_j][:, None, :]  6.88 us
    transpose x1, local copies, waits for them, and re-layouts, shards(): jnp.swapaxes(blocks, 2, 3)  6.29 us
  transfers between devices with their start and end apart: 1, of which 1 were waited for; matrix products, arithmetic and copies ran while one was open for 31% of the time, Pallas kernels for 0%

commit v1 on v0

--- a/solution.py
+++ b/solution.py
@@ -2,6 +2,18 @@
 import jax.numpy as jnp
 from jax import lax
 from jax.sharding import PartitionSpec as P
+
+
+def collect(x, axis, dim):
+    ways, here = (lax.axis_size(axis), lax.axis_index(axis))
+    grown, reach = (x, 1)
+    while reach < ways:
+        theirs = lax.ppermute(grown, axis, [(d, d ^ reach) for d in range(ways)])
+        mine_first = jnp.concatenate([grown, theirs], axis=dim)
+        theirs_first = jnp.concatenate([theirs, grown], axis=dim)
+        grown = jnp.where(here & reach == 0, mine_first, theirs_first)
+        reach = 2 * reach
+    return grown
 
 
 def one_hot(ids, width):
@@ -34,7 +46,7 @@
     aux_index = lax.axis_index("aux")
     half_rows = extent // halves
     row_first = aux_index * half_rows
-    every_amp = lax.all_gather(amplitudes, "orb", axis=0, tiled=True)
+    every_amp = collect(amplitudes, "orb", 0)
     own_slots = owner_index * slot_count + jnp.arange(slot_count, dtype=jnp.int32)
     orb_i = pair_slot_orbitals[own_slots, 0]
     orb_j = pair_slot_orbitals[own_slots, 1]

time: 167 us -> 596 us (3.57)
  waiting for transfers between devices: 68.8 us -> 476 us
  other arithmetic: 0.11 us -> 35.1 us
  between operations: 14.4 us -> 1.03 us
  starting transfers between devices: 0.04 us -> 9.02 us
  local copies, waits for them, and re-layouts: 48.3 us -> 40.8 us
    ppermute x0 -> x5, waiting for transfers between devices: none -> 476 us  [collect(): theirs = lax.ppermute(grown, axis, [(d, d ^ reach) for d in range(ways)])]
    all_gather x1 -> x0, waiting for transfers between devices: 68.1 us -> none  [shards(): every_amp = lax.all_gather(amplitudes, 'orb', axis=0, tiled=True)]
    select_n x0 -> x5, other arithmetic: none -> 34.9 us  [collect(): grown = jnp.where(here & reach == 0, mine_first, theirs_first)]
    ppermute x0 -> x5, starting transfers between devices: none -> 9.02 us  [collect(): theirs = lax.ppermute(grown, axis, [(d, d ^ reach) for d in range(ways)])]
  transfers between devices with their start and end apart: 1 -> 5, of which waited for: 1 -> 5; matrix products, arithmetic and copies ran while one was open for 31% -> 7% of each run, Pallas kernels for 0% -> 0%
where the time goes in v1:
time: 596 us
  waiting for transfers between devices  476 us (80%)
  local copies, waits for them, and re-layouts  40.8 us (7%)
  other arithmetic  35.1 us (6%)
  matrix products  34.3 us (6%)
  starting transfers between devices  9.02 us (2%)
    ppermute x5, waiting for transfers between devices, collect(): theirs = lax.ppermute(grown, axis, [(d, d ^ reach) for d in range(ways)])  476 us
    select_n x5, other arithmetic, collect(): grown = jnp.where(here & reach == 0, mine_first, theirs_first)  34.9 us
  transfers between devices with their start and end apart: 5, of which 5 were waited for; matrix products, arithmetic and copies ran while one was open for 7% of the time, Pallas kernels for 0%

profile of v1, /device:TPU:0, one launch (start us, length us, event | category | flops | bytes accessed | tf_op | source)
XLA Modules:
  0.0 596.0 jit_solution(4998061952478820700)
XLA Ops:
  1.2 1.7 collective-permute-done
  2.9 1.4 maximum_select_fusion.4
  4.3 2.9 collective-permute-start.1
  7.3 23.6 %collective-permute-done.1 = bf16[8,256,256]{2,1,0:T(8,128)(2,1)} collective-permute-done((bf16[8,256,256]{2,1,0:T(8,128)(2,1)S(1)}, bf16[8,256,256]{2,1,0:T(8,128)(2,1)}, u32[]{:S(2)}, u32[]{:S(2)}) %collective-permute-start.1) | collective-permute-done | bytes 1048608 | tf_op jit(solution)/shard_map/ppermute | solution.py:11
  30.8 2.8 maximum_select_fusion.3
  33.6 1.8 collective-permute-start.2
  35.5 45.5 %collective-permute-done.2 = bf16[16,256,256]{2,1,0:T(8,128)(2,1)} collective-permute-done((bf16[16,256,256]{2,1,0:T(8,128)(2,1)S(1)}, bf16[16,256,256]{2,1,0:T(8,128)(2,1)}, u32[]{:S(2)}, u32[]{:S(2)}) %collective-permute-start.2) | collective-permute-done | bytes 2097184 | tf_op jit(solution)/shard_map/ppermute | solution.py:11
  81.0 3.9 maximum_select_fusion.2
  84.8 1.5 collective-permute-start.3
  86.4 90.0 %collective-permute-done.3 = bf16[32,256,256]{2,1,0:T(8,128)(2,1)} collective-permute-done((bf16[32,256,256]{2,1,0:T(8,128)(2,1)}, bf16[32,256,256]{2,1,0:T(8,128)(2,1)}, u32[]{:S(2)}, u32[]{:S(2)}) %collective-permute-start.3) | collective-permute-done | bytes 4194336 | tf_op jit(solution)/shard_map/ppermute | solution.py:11
  176.4 9.3 %maximum_select_fusion.1 = bf16[64,256,256]{2,1,0:T(8,128)(2,1)} fusion(bf16[32,256,256]{2,1,0:T(8,128)(2,1)} %collective-permute-done.3, bf16[32,256,256]{2,1,0:T(8,128)(2,1)} %maximum_select_fusion.2, pred[]{:T(512)S(6)} %eq.92), kind=kLoop, calls=%fused_computation.19 | loop fusion | flops 12582912 | bytes 16777216 | tf_op jit(solution)/shard_map/jit(_where)/select_n | solution.py:14
  185.6 2.2 collective-permute-start.4
  195.1 4.8 gather_fusion.11
  200.0 6.9 %gather_fusion.12 = f32[1024]{0:T(1024)S(1)} fusion(f32[512]{0:T(512)S(1)} %convert_element_type.73, s32[1024]{0:T(1024)S(1)} %broadcast_clamp_fusion.1), kind=kCustom, calls=%fused_computation.12 | custom fusion | bytes 12288 | tf_op jit(solution)/shard_map/gather | solution.py:116
  206.9 6.9 %gather_fusion.13 = f32[1024]{0:T(1024)S(1)} fusion(f32[512]{0:T(512)S(1)} %convert_element_type.73, s32[1024]{0:T(1024)S(1)} %broadcast_clamp_fusion), kind=kCustom, calls=%fused_computation.13 | custom fusion | bytes 12288 | tf_op jit(solution)/shard_map/gather | solution.py:116
  214.1 1.7 fusion.28.clone.5
  217.0 1.1 fusion.38
  218.1 1.9 fusion.41
  220.0 1.7 fusion.24
  221.7 2.0 convolution_convert_fusion
  223.8 1.7 convolution_add_fusion.1
  225.4 1.4 convolution_add_fusion
  227.2 4.6 fusion.13
  231.8 315.1 %collective-permute-done.4 = bf16[64,256,256]{2,1,0:T(8,128)(2,1)} collective-permute-done((bf16[64,256,256]{2,1,0:T(8,128)(2,1)}, bf16[64,256,256]{2,1,0:T(8,128)(2,1)}, u32[]{:S(2)}, u32[]{:S(2)}) %collective-permute-start.4) | collective-permute-done | bytes 8388640 | tf_op jit(solution)/shard_map/ppermute | solution.py:11
  546.8 17.6 %maximum_select_fusion = bf16[128,256,256]{2,1,0:T(8,128)(2,1)} fusion(bf16[64,256,256]{2,1,0:T(8,128)(2,1)} %collective-permute-done.4, bf16[64,256,256]{2,1,0:T(8,128)(2,1)} %maximum_select_fusion.1, pred[]{:T(512)S(6)} %eq.91), kind=kLoop, calls=%fused_computation.14 | loop fusion | flops 25165824 | bytes 33554432 | tf_op jit(solution)/shard_map/jit(_where)/select_n | solution.py:14
  564.4 8.5 %gather_fusion.9 = bf16[32,256,256]{2,1,0:T(8,128)(2,1)} fusion(bf16[128,256,256]{2,1,0:T(8,128)(2,1)} %maximum_select_fusion, s32[1024]{0:T(1024)S(1)} %pad_clamp_fusion.1), kind=kCustom, calls=%fused_computation.9 | custom fusion | bytes 8388736 | tf_op jit(solution)/shard_map/gather | solution.py:105
  573.0 6.3 %copy.14 = bf16[4,8,256,256]{3,2,1,0:T(8,128)(2,1)} copy(bf16[4,8,256,256]{2,3,1,0:T(8,128)(2,1)} %bitcast.131) | data formatting | bytes 8388608 | tf_op jit(solution)/shard_map/transpose | solution.py:106
  579.3 8.6 %fusion.8 = bf16[4,8,256,256]{3,2,1,0:T(8,128)(2,1)} fusion(bf16[4,8,256,256]{3,2,1,0:T(8,128)(2,1)} %copy.14, bf16[4,8,256,256]{3,2,1,0:T(8,128)(2,1)} %bitcast.132, pred[4,8]{1,0:T(4,128)(4,1)S(1)} %get-tuple-element.11, s32[4,8,256]{2,1,0:T(8,128)S(1)} %bitcast.133, bf16[4,256,512]{2,1,0:T(8,128)(2,1)S(1)} %copy-done.14), kind=kOutput, calls=%fused_computation.27 | convolution fusion | flops 3231711232 | bytes 13664288 | tf_op jit(solution)/shard_map/bcrp,bcpd->bcrd/dot_general | solution.py:107
  587.9 1.7 fusion.36
  589.5 2.3 fusion.35
  591.8 1.4 fusion.34
  594.4 1.6 subtract_convert_fusion
  (80 shorter events, 10.7 us)
Async XLA Ops:
  0.6 213.5 %copy-start = (bf16[512,512]{1,0:T(8,128)(2,1)S(1)}, bf16[512,512]{1,0:T(8,128)(2,1)}, u32[]{:S(2)}) copy-start(bf16[512,512]{1,0:T(8,128)(2,1)} %param.15) | copy-start | bytes 1572868
  0.6 2.3 collective-permute-start
  4.3 2.9 copy-start.5
  4.3 26.5 %collective-permute-start.1 = (bf16[8,256,256]{2,1,0:T(8,128)(2,1)S(1)}, bf16[8,256,256]{2,1,0:T(8,128)(2,1)}, u32[]{:S(2)}, u32[]{:S(2)}) collective-permute-start(bf16[8,256,256]{2,1,0:T(8,128)(2,1)S(1)} %maximum_select_fusion.4), channel_id=1, source_target_pairs={{0,2},{1,3},{2,0},{3,1},{4,6},{5,7},{6,4},{7,5},{8,10},{9,11},{10,... | collective-permute-start | bytes 3145736 | tf_op jit(solution)/shard_map/ppermute | solution.py:11
  33.6 47.3 %collective-permute-start.2 = (bf16[16,256,256]{2,1,0:T(8,128)(2,1)S(1)}, bf16[16,256,256]{2,1,0:T(8,128)(2,1)}, u32[]{:S(2)}, u32[]{:S(2)}) collective-permute-start(bf16[16,256,256]{2,1,0:T(8,128)(2,1)S(1)} %maximum_select_fusion.3), channel_id=1, source_target_pairs={{0,4},{1,5},{2,6},{3,7},{4,0},{5,1},{6,2},{7,3},{8,12},{9,13},{10,... | collective-permute-start | bytes 6291464 | tf_op jit(solution)/shard_map/ppermute | solution.py:11
  84.8 91.5 %collective-permute-start.3 = (bf16[32,256,256]{2,1,0:T(8,128)(2,1)}, bf16[32,256,256]{2,1,0:T(8,128)(2,1)}, u32[]{:S(2)}, u32[]{:S(2)}) collective-permute-start(bf16[32,256,256]{2,1,0:T(8,128)(2,1)} %maximum_select_fusion.2), channel_id=1, source_target_pairs={{0,8},{1,9},{2,10},{3,11},{4,12},{5,13},{6,14},{7,15},{8,0},{9,1},... | collective-permute-start | bytes 12582920 | tf_op jit(solution)/shard_map/ppermute | solution.py:11
  86.4 101.5 %copy-start.2 = (s32[128,2]{0,1:T(2,128)S(1)}, s32[128,2]{0,1:T(2,128)}, u32[]{:S(2)}) copy-start(s32[128,2]{0,1:T(2,128)} %param.13) | copy-start | bytes 3076
  86.4 102.8 %copy-start.4 = (s32[64,256]{1,0:T(8,128)S(1)}, s32[64,256]{1,0:T(8,128)}, u32[]{:S(2)}) copy-start(s32[64,256]{1,0:T(8,128)} %param.14) | copy-start | bytes 196612
  86.4 104.0 %copy-start.3 = (f32[64]{0:T(128)S(1)}, f32[64]{0:T(128)}, u32[]{:S(2)}) copy-start(f32[64]{0:T(128)} %param.17) | copy-start | bytes 772
  86.4 105.3 %copy-start.12 = (s32[4,8]{1,0:T(4,128)S(1)}, s32[4,8]{1,0:T(4,128)}, u32[]{:S(2)}) copy-start(s32[4,8]{1,0:T(4,128)} %param.19) | copy-start | bytes 388
  86.4 105.3 %copy-start.13 = (s32[4,8]{1,0:T(4,128)S(1)}, s32[4,8]{1,0:T(4,128)}, u32[]{:S(2)}) copy-start(s32[4,8]{1,0:T(4,128)} %param.18) | copy-start | bytes 388
  185.6 8.0 %copy-start.11 = (s32[4,8]{1,0:T(4,128)S(1)}, s32[4,8]{1,0:T(4,128)}, u32[]{:S(2)}) copy-start(s32[4,8]{1,0:T(4,128)} %param.20) | copy-start | bytes 388
  185.6 9.4 %copy-start.9 = (bf16[512,512]{1,0:T(8,128)(2,1)S(1)}, bf16[512,512]{1,0:T(8,128)(2,1)}, u32[]{:S(2)}) copy-start(bf16[512,512]{1,0:T(8,128)(2,1)} %param.16) | copy-start | bytes 1572868
  185.6 361.2 %collective-permute-start.4 = (bf16[64,256,256]{2,1,0:T(8,128)(2,1)}, bf16[64,256,256]{2,1,0:T(8,128)(2,1)}, u32[]{:S(2)}, u32[]{:S(2)}) collective-permute-start(bf16[64,256,256]{2,1,0:T(8,128)(2,1)} %maximum_select_fusion.1), channel_id=1, source_target_pairs={{0,16},{1,17},{2,18},{3,19},{4,20},{5,21},{6,22},{7,23},{8,24},{9,... | collective-permute-start | bytes 25165832 | tf_op jit(solution)/shard_map/ppermute | solution.py:11
  199.9 13.8 %copy-start.10 = (f32[4,8]{1,0:T(4,128)S(1)}, f32[4,8]{1,0:T(4,128)}, u32[]{:S(2)}) copy-start(f32[4,8]{1,0:T(4,128)} %param.21) | copy-start | bytes 388
  218.1 3.7 copy-start.8
  225.4 1.8 copy-start.15
  573.0 6.3 %copy-start.14 = (bf16[4,256,512]{2,1,0:T(8,128)(2,1)S(1)}, bf16[4,256,512]{2,1,0:T(8,128)(2,1)}, u32[]{:S(2)}) copy-start(bf16[4,256,512]{2,1,0:T(8,128)(2,1)} %fusion.24) | copy-start | bytes 3145732
  587.8 3.9 copy-start.6
  587.9 5.3 copy-start.7
  594.1 1.9 copy-start.1
